TPU v7x, 128 devices: a whole 4x4x4 slice. The times are simulated.
128 devices in a mesh: section: 16 (over z_lo, x, core), ctx: 8 (over z_hi, y).
Axes of the slice: x: 4, y: 4, z: 4 (z_hi: 2, z_lo: 2; z = z_hi * 2 + z_lo), core: 2. Of those that a mesh axis runs over, the one named last changes fastest.
Arguments:
- sent_fwd: bfloat16 [16, 1024, 4096], P('section', 'ctx'), may hold values from -6 to 6
- sent_grad: bfloat16 [16, 1024, 4096], P('section', 'ctx'), may hold values from -6 to 6
- saved_bwd: bfloat16 [16, 1024, 4096], P('section', 'ctx'), may hold values from -6 to 6
- norm_gain: float32 [16, 4096], P('section'), may hold values from 0.5 to 1.5
- key_proj: bfloat16 [16, 4096, 512], P('section')
- value_proj: bfloat16 [16, 4096, 512], P('section'), may hold values from -0.09375 to 0.09375
- seg_fwd: int32 [1024], replicated, may hold values from 0 to 3, never falling along the last dimension, each value on 1 to 512 neighbouring positions
- seg_bwd: int32 [1024], replicated, may hold values from 0 to 3, never falling along the last dimension, each value on 1 to 512 neighbouring positions
Outputs:
- fwd_out: bfloat16 [16, 1024, 4096], P('section', 'ctx')
- grad_out: bfloat16 [16, 1024, 4096], P('section', 'ctx')
Inputs may be any that keep to these rules, and one draw needn't show every extreme that they name: `seg_fwd`: segment ids never fall along the sequence, each segment has 1 to 512 positions and one has exactly 512. `seg_bwd`: segment ids never fall along the sequence, each segment has 1 to 512 positions and one has exactly 512.
All inputs are finite; a program needn't handle non-finite values.
Results may differ from a plain program's by a relative error of at most 0.02.
The roundings to bfloat16 on the way count: a program that leaves them out, or rounds other values in their place, can miss the bound.
Values may be sent and summed in bfloat16 or wider, within the bound.
No kernel may reach another device: no remote copies, remote signals or barrier semaphores. Data moves between devices by JAX's collectives and lax.ppermute only.
A program may use at most 128 MiB of HBM per device.

v0:
```python
import jax
import jax.numpy as jnp
from jax import lax
from jax.sharding import PartitionSpec as P

HD = 128
EPSILON = 1e-05
NEGATIVE = -1e30


def shifted(block, axis, distance):
    devices = range(lax.axis_size(axis))
    route = [((i - distance) % len(devices), i) for i in devices]
    return lax.ppermute(block, axis, route)


def normalize(inputs, gain):
    wide = inputs.astype(jnp.float32)
    inverse = lax.rsqrt(jnp.mean(wide * wide, axis=-1, keepdims=True) + EPSILON)
    return (wide * inverse * gain, wide, inverse)


def body(sent_fwd, sent_grad, saved_bwd, norm_gain, key_proj, value_proj, seg_fwd, seg_bwd):
    tok_rows = sent_fwd.shape[1]
    width = sent_fwd.shape[2]
    kv_width = key_proj.shape[2]
    heads = width // HD
    kv_heads = kv_width // HD
    group_size = heads // kv_heads
    scale_factor = HD ** (-0.5)
    offset = lax.axis_index("ctx") * tok_rows
    query_pos = offset + jnp.arange(tok_rows, dtype=jnp.int32)
    gain = norm_gain[0]
    key_weight = key_proj[0]
    value_weight = value_proj[0]
    arrived = shifted(sent_fwd, "section", 1)[0]
    upstream = shifted(sent_grad, "section", -1)[0]

    def layer_parts(inputs):
        normed, wide, inverse = normalize(inputs, gain)
        flat = normed.astype(jnp.bfloat16)
        keys = jnp.dot(flat, key_weight, preferred_element_type=jnp.float32).astype(jnp.bfloat16)
        values = jnp.dot(flat, value_weight, preferred_element_type=jnp.float32).astype(
            jnp.bfloat16
        )
        return (flat.reshape(tok_rows, heads, HD), keys, values, wide, inverse)

    fwd_query, fwd_keys, fwd_values, fwd_wide, fwd_inverse = layer_parts(arrived)
    bwd_query, bwd_keys, bwd_values, bwd_wide, bwd_inverse = layer_parts(saved_bwd[0])
    seg_query_fwd = lax.dynamic_slice_in_dim(seg_fwd, offset, tok_rows)
    key_piece = lax.all_gather(fwd_keys, "ctx", axis=0, tiled=True)
    value_piece = lax.all_gather(fwd_values, "ctx", axis=0, tiled=True)
    count_rows = key_piece.shape[0]
    key_pos = jnp.arange(count_rows, dtype=jnp.int32)
    allowed = (key_pos[None, :] <= query_pos[:, None]) & (
        seg_query_fwd[:, None] == seg_fwd[None, :]
    )
    run_max = jnp.full((heads, tok_rows), NEGATIVE, jnp.float32)
    new_max = []
    new_total = []
    new_acc = []
    for forward_group_idx in range(kv_heads):
        forward_head_slice = slice(
            forward_group_idx * group_size, (forward_group_idx + 1) * group_size
        )
        forward_feat_slice = slice(forward_group_idx * HD, (forward_group_idx + 1) * HD)
        forward_scores = (
            jnp.einsum(
                "tgd,sd->gts",
                fwd_query[:, forward_head_slice],
                key_piece[:, forward_feat_slice],
                preferred_element_type=jnp.float32,
            )
            * scale_factor
        )
        forward_scores = jnp.where(allowed[None], forward_scores, NEGATIVE)
        old_max = run_max[forward_head_slice]
        top_max = jnp.maximum(old_max, jnp.max(forward_scores, axis=-1))
        forward_expo = jnp.where(allowed[None], jnp.exp(forward_scores - top_max[:, :, None]), 0.0)
        new_max.append(top_max)
        new_total.append(jnp.sum(forward_expo, axis=-1))
        product = jnp.einsum(
            "gts,sd->gtd",
            forward_expo.astype(jnp.bfloat16),
            value_piece[:, forward_feat_slice],
            preferred_element_type=jnp.float32,
        )
        new_acc.append(product)
    bwd_key_all, bwd_value_all = (
        lax.all_gather(bwd_keys, "ctx", axis=0, tiled=True),
        lax.all_gather(bwd_values, "ctx", axis=0, tiled=True),
    )
    attended = jnp.concatenate(new_acc, axis=0) / jnp.concatenate(new_total, axis=0)[:, :, None]
    attended = jnp.transpose(attended, (1, 0, 2)).reshape(tok_rows, width)
    fwd_out = (arrived.astype(jnp.float32) + attended).astype(jnp.bfloat16)
    seq_len = bwd_key_all.shape[0]
    key_pos = jnp.arange(seq_len, dtype=jnp.int32)
    seg_query_bwd = lax.dynamic_slice_in_dim(seg_bwd, offset, tok_rows)
    allowed = (key_pos[None, :] <= query_pos[:, None]) & (
        seg_query_bwd[:, None] == seg_bwd[None, :]
    )
    grad_heads = upstream.reshape(tok_rows, heads, HD)
    dquery_parts, dkey_parts, dvalue_parts = ([], [], [])
    for group_idx in range(kv_heads):
        head_slice = slice(group_idx * group_size, (group_idx + 1) * group_size)
        feat_slice = slice(group_idx * HD, (group_idx + 1) * HD)
        query_grp = bwd_query[:, head_slice]
        key_grp = bwd_key_all[:, feat_slice]
        value_grp = bwd_value_all[:, feat_slice]
        grad_grp = grad_heads[:, head_slice]
        scores = (
            jnp.einsum("tgd,sd->gts", query_grp, key_grp, preferred_element_type=jnp.float32)
            * scale_factor
        )
        scores = jnp.where(allowed[None], scores, NEGATIVE)
        rowmax = jnp.max(scores, axis=-1, keepdims=True)
        expo = jnp.where(allowed[None], jnp.exp(scores - rowmax), 0.0)
        total = jnp.sum(expo, axis=-1, keepdims=True)
        probs = expo / total
        dprob = jnp.einsum("tgd,sd->gts", grad_grp, value_grp, preferred_element_type=jnp.float32)
        delta = jnp.sum(probs * dprob, axis=-1, keepdims=True)
        dscore_b = (probs * (dprob - delta)).astype(jnp.bfloat16)
        dquery_parts.append(
            jnp.einsum("gts,sd->tgd", dscore_b, key_grp, preferred_element_type=jnp.float32)
            * scale_factor
        )
        probs_b = probs.astype(jnp.bfloat16)
        dkey_parts.append(
            jnp.einsum("gts,tgd->sd", dscore_b, query_grp, preferred_element_type=jnp.float32)
            * scale_factor
        )
        dvalue_parts.append(
            jnp.einsum("gts,tgd->sd", probs_b, grad_grp, preferred_element_type=jnp.float32)
        )
    dquery = jnp.concatenate(dquery_parts, axis=1).reshape(tok_rows, width)
    dkey_terms = jnp.concatenate(dkey_parts, axis=1)
    dvalue_terms = jnp.concatenate(dvalue_parts, axis=1)
    dkeys, dvalues = (
        lax.psum_scatter(
            dkey_terms.astype(jnp.bfloat16), "ctx", scatter_dimension=0, tiled=True
        ).astype(jnp.float32),
        lax.psum_scatter(
            dvalue_terms.astype(jnp.bfloat16), "ctx", scatter_dimension=0, tiled=True
        ).astype(jnp.float32),
    )
    dnormed = dquery + jnp.dot(
        dkeys.astype(jnp.bfloat16), jnp.transpose(key_weight), preferred_element_type=jnp.float32
    )
    dnormed = dnormed + jnp.dot(
        dvalues.astype(jnp.bfloat16),
        jnp.transpose(value_weight),
        preferred_element_type=jnp.float32,
    )
    scaled = gain * dnormed
    grad_in = bwd_inverse * scaled - bwd_wide * bwd_inverse**3 * jnp.mean(
        bwd_wide * scaled, axis=-1, keepdims=True
    )
    grad_out = (upstream.astype(jnp.float32) + grad_in).astype(jnp.bfloat16)
    return (fwd_out[None], grad_out[None])


def solution(mesh):
    placed = (
        P("section", "ctx", None),
        P("section", "ctx", None),
        P("section", "ctx", None),
        P("section", None),
        P("section", None, None),
        P("section", None, None),
        P(),
        P(),
    )
    return jax.shard_map(
        body,
        mesh=mesh,
        in_specs=placed,
        out_specs=(P("section", "ctx", None), P("section", "ctx", None)),
        check_vma=False,
    )
```

profile of v0, /device:TPU:0, one launch (start us, length us, event | category | flops | bytes accessed | tf_op | source)
XLA Modules:
  0.0 373.6 jit_solution(17284572037392446250)
XLA Ops:
  9.5 3.9 %fusion.121 = bf16[128,512]{1,0:T(8,128)(2,1)} fusion(bf16[1,4096,512]{2,1,0:T(8,128)(2,1)} %param.12, bf16[1,128,4096]{2,1,0:T(8,128)(2,1)} %param.10, f32[128]{0:T(128)S(1)} %get-tuple-element.12, f32[4096]{0:T(1024)} %bitcast.352), kind=kOutput, calls=%fused_computation.149 | convolution fusion | flops 539033600 | bytes 5390848 | tf_op jit(solution)/shard_map/dot_general | solution.py:42
  13.6 3.6 fusion.127
  17.3 12.7 %collective-permute-done = bf16[1,128,4096]{2,1,0:T(8,128)(2,1)S(1)} collective-permute-done((bf16[1,128,4096]{2,1,0:T(8,128)(2,1)S(1)}, bf16[1,128,4096]{2,1,0:T(8,128)(2,1)S(1)}, u32[]{:S(2)}, u32[]{:S(2)}) %collective-permute-start) | collective-permute-done | bytes 1048608 | tf_op jit(solution)/shard_map/ppermute | solution.py:14
  30.3 3.6 fusion.118
  35.9 2.9 copy.40
  40.8 2.9 copy.29
  43.7 3.6 fusion.124
  47.4 4.2 %multiply_convert_fusion = (bf16[128,32,128]{2,0,1:T(8,128)(2,1)}, bf16[128,32,128]{2,0,1:T(8,128)(2,1)}) fusion(f32[128,32,128]{2,0,1:T(8,128)} %copy.40, f32[128]{0:T(128)S(1)} %get-tuple-element.12, f32[32,128]{1,0:T(8,128)S(1)} %bitcast.356, f32[128,32,128]{2,0,1:T(8,128)} %copy.29, f32[128]{0:T(128)S(1)} %add_rsqrt_fusion.1), kind=kLoop, calls=%fused_computation.95 | loop fusion | flops 3145728 | bytes 6308864 | tf_op jit(solution)/shard_map/convert_element_type | solution.py:41
  53.4 10.2 %all-gather.9.cloned.1.call-done = bf16[1024,512]{1,0:T(8,128)(2,1)} async-done(((bf16[128,512]{1,0:T(8,128)(2,1)}), bf16[1024,512]{1,0:T(8,128)(2,1)}) %all-gather.9.cloned.1.call-update) | async-done | bytes 1048592 | tf_op jit(solution)/shard_map/all_gather | solution.py:90
  63.6 4.7 %fusion.224 = (f32[8,128]{1,0:T(8,128)S(1)}, f32[8,128,1024]{1,2,0:T(8,128)}) fusion(pred[128,1024]{0,1:T(8,128)(4,1)S(1)} %get-tuple-element.13, bf16[128,32,128]{2,0,1:T(8,128)(2,1)} %get-tuple-element.9, bf16[1024,512]{1,0:T(8,128)(2,1)} %all-gather.9.cloned.1.call-done), kind=kOutput, calls=%fused_computation.247 | convolution fusion | flops 273679360 | bytes 4984832 | tf_op jit(solution)/shard_map/sub | solution.py:117
  68.3 44.6 %all-gather.11.cloned.1.call-done = bf16[1024,512]{1,0:T(8,128)(2,1)} async-done(((bf16[128,512]{1,0:T(8,128)(2,1)}), bf16[1024,512]{1,0:T(8,128)(2,1)}) %all-gather.11.cloned.1.call-update) | async-done | bytes 1048592 | tf_op jit(solution)/shard_map/all_gather | solution.py:91
  112.9 3.2 fusion.8
  120.1 5.5 %fusion.219 = (f32[8,128]{1,0:T(8,128)}, f32[8,128,1024]{1,2,0:T(8,128)}) fusion(pred[128,1024]{0,1:T(8,128)(4,1)} %copy-done.26, bf16[128,32,128]{2,0,1:T(8,128)(2,1)} %get-tuple-element.9, bf16[1024,512]{1,0:T(8,128)(2,1)} %all-gather.9.cloned.1.call-done), kind=kOutput, calls=%fused_computation.246 | convolution fusion | flops 273679360 | bytes 4984832 | tf_op jit(solution)/shard_map/sub | solution.py:117
  125.5 3.2 fusion.5
  131.0 2.4 fusion.117
  133.4 5.4 %fusion.229 = (f32[8,128]{1,0:T(8,128)}, f32[8,128,1024]{1,2,0:T(8,128)}) fusion(pred[128,1024]{0,1:T(8,128)(4,1)} %copy-done.26, bf16[128,32,128]{2,0,1:T(8,128)(2,1)} %get-tuple-element.9, bf16[1024,512]{1,0:T(8,128)(2,1)} %all-gather.9.cloned.1.call-done), kind=kOutput, calls=%fused_computation.248 | convolution fusion | flops 273679360 | bytes 4984832 | tf_op jit(solution)/shard_map/sub | solution.py:117
  138.8 3.2 fusion.11
  144.3 5.4 %fusion.234 = (f32[8,128]{1,0:T(8,128)}, f32[8,128,1024]{1,2,0:T(8,128)}) fusion(pred[128,1024]{0,1:T(8,128)(4,1)} %copy-done.26, bf16[128,32,128]{2,0,1:T(8,128)(2,1)} %get-tuple-element.9, bf16[1024,512]{1,0:T(8,128)(2,1)} %all-gather.9.cloned.1.call-done), kind=kOutput, calls=%fused_computation.249 | convolution fusion | flops 273679360 | bytes 4984832 | tf_op jit(solution)/shard_map/sub | solution.py:117
  149.8 3.4 fusion.14
  158.1 2.9 fusion.105
  168.2 2.9 copy.54
  171.1 3.2 fusion.102
  183.1 2.9 fusion.35
  187.9 3.2 fusion.37
  191.2 18.2 %all-gather.7.cloned.1.call-done = bf16[1024,512]{1,0:T(8,128)(2,1)} async-done(((bf16[128,512]{1,0:T(8,128)(2,1)}), bf16[1024,512]{1,0:T(8,128)(2,1)}) %all-gather.7.cloned.1.call-update) | async-done | bytes 1048592 | tf_op jit(solution)/shard_map/all_gather | solution.py:52
  209.4 3.5 fusion.72
  220.2 3.0 copy.38
  223.2 2.8 add_convert_fusion
  226.0 59.2 %reduce-scatter.3.cloned.1.call-done = bf16[128,512]{1,0:T(8,128)(2,1)} async-done(((bf16[1024,512]{1,0:T(8,128)(2,1)}), bf16[128,512]{1,0:T(8,128)(2,1)}) %reduce-scatter.3.cloned.1.call-update) | async-done | bytes 131088 | tf_op jit(solution)/shard_map/reduce_scatter | solution.py:139
  285.1 5.7 %convolution_add_fusion.1 = f32[128,4096]{1,0:T(8,128)} fusion(f32[128,4096]{1,0:T(8,128)} %copy.54, bf16[128,512]{1,0:T(8,128)(2,1)} %reduce-scatter.3.cloned.1.call-done, bf16[1,4096,512]{2,1,0:T(8,128)(2,1)} %param.12), kind=kOutput, calls=%fused_computation.6 | convolution fusion | flops 537395200 | bytes 8519680 | tf_op jit(solution)/shard_map/dot_general | solution.py:146
  290.9 69.5 %reduce-scatter.5.cloned.1.call-done = bf16[128,512]{1,0:T(8,128)(2,1)} async-done(((bf16[1024,512]{1,0:T(8,128)(2,1)}), bf16[128,512]{1,0:T(8,128)(2,1)}) %reduce-scatter.5.cloned.1.call-update) | async-done | bytes 131088 | tf_op jit(solution)/shard_map/reduce_scatter | solution.py:142
  360.4 4.5 %fusion.47 = (f32[128]{0:T(128)S(1)}, f32[128,4096]{1,0:T(8,128)S(1)}) fusion(bf16[1,128,4096]{2,1,0:T(8,128)(2,1)S(1)} %copy-done, f32[128,4096]{1,0:T(8,128)} %convolution_add_fusion.1, bf16[128,512]{1,0:T(8,128)(2,1)} %reduce-scatter.5.cloned.1.call-done, bf16[1,4096,512]{2,1,0:T(8,128)(2,1)} %param.13, f32[4096]{0:T(1024)S(1)} %bitcast.357), kind=kOutput, calls=%fused_computation.79 | convolution fusion | flops 539492224 | bytes 9585152 | tf_op jit(solution)/shard_map/dot_general | solution.py:149
  (138 shorter events, 48.5 us)
Async XLA Ops:
  7.2 6.4 %copy-start = (bf16[1,128,4096]{2,1,0:T(8,128)(2,1)S(1)}, bf16[1,128,4096]{2,1,0:T(8,128)(2,1)}, u32[]{:S(2)}) copy-start(bf16[1,128,4096]{2,1,0:T(8,128)(2,1)} %param.10) | copy-start | bytes 3145732
  7.2 6.4 %copy-start.27 = (f32[1,4096]{1,0:T(1,128)S(1)}, f32[1,4096]{1,0:T(1,128)}, u32[]{:S(2)}) copy-start(f32[1,4096]{1,0:T(1,128)} %param.11) | copy-start | bytes 49156
  7.2 6.3 %copy-start.39 = (bf16[1,128,4096]{2,1,0:T(8,128)(2,1)S(1)}, bf16[1,128,4096]{2,1,0:T(8,128)(2,1)}, u32[]{:S(2)}) copy-start(bf16[1,128,4096]{2,1,0:T(8,128)(2,1)} %param.8) | copy-start | bytes 3145732
  7.2 56.4 %all-gather.9.cloned.1.call-start = ((), (), s32[]{:S(2)}) async-start(), calls=%async_computation.4 | async-start | bytes 1179648 | tf_op jit(solution)/shard_map/all_gather | solution.py:90
  9.5 37.9 %copy-start.36 = (f32[128]{0:T(128)}, f32[128]{0:T(128)S(1)}, u32[]{:S(2)}) copy-start(f32[128]{0:T(128)S(1)} %get-tuple-element.12) | copy-start | bytes 1540
  13.4 99.4 %all-gather.11.cloned.1.call-start = ((), (), s32[]{:S(2)}) async-start(), calls=%async_computation.5 | async-start | bytes 1179648 | tf_op jit(solution)/shard_map/all_gather | solution.py:91
  13.5 16.5 %collective-permute-start = (bf16[1,128,4096]{2,1,0:T(8,128)(2,1)S(1)}, bf16[1,128,4096]{2,1,0:T(8,128)(2,1)S(1)}, u32[]{:S(2)}, u32[]{:S(2)}) collective-permute-start(bf16[1,128,4096]{2,1,0:T(8,128)(2,1)S(1)} %copy-done.39), channel_id=1, source_target_pairs={{120,0},{0,8},{8,16},{16,24},{24,32},{32,40},{40,48},{48,56},{56,6... | collective-permute-start | bytes 3145736 | tf_op jit(solution)/shard_map/ppermute | solution.py:14
  17.2 161.9 %all-gather.5.cloned.1.call-start = ((), (), s32[]{:S(2)}) async-start(), calls=%async_computation.2 | async-start | bytes 1179648 | tf_op jit(solution)/shard_map/all_gather | solution.py:51
  30.3 5.4 %copy-start.29 = (s32[1024]{0:T(1024)S(1)}, s32[1024]{0:T(1024)}, u32[]{:S(2)}) copy-start(s32[1024]{0:T(1024)} %param.14) | copy-start | bytes 12292
  30.3 5.5 %copy-start.28 = (s32[1024]{0:T(1024)S(1)}, s32[1024]{0:T(1024)}, u32[]{:S(2)}) copy-start(s32[1024]{0:T(1024)} %param.15) | copy-start | bytes 12292
  34.0 175.4 %all-gather.7.cloned.1.call-start = ((), (), s32[]{:S(2)}) async-start(), calls=%async_computation.3 | async-start | bytes 1179648 | tf_op jit(solution)/shard_map/all_gather | solution.py:52
  34.0 17.6 %collective-permute-start.1 = (bf16[1,128,4096]{2,1,0:T(8,128)(2,1)}, bf16[1,128,4096]{2,1,0:T(8,128)(2,1)S(1)}, u32[]{:S(2)}, u32[]{:S(2)}) collective-permute-start(bf16[1,128,4096]{2,1,0:T(8,128)(2,1)} %param.9), channel_id=1, source_target_pairs={{8,0},{16,8},{24,16},{32,24},{40,32},{48,40},{56,48},{64,56},{72,6... | collective-permute-start | bytes 3145736 | tf_op jit(solution)/shard_map/ppermute | solution.py:14
  39.2 24.4 %copy-start.26 = (pred[128,1024]{0,1:T(8,128)(4,1)}, pred[128,1024]{0,1:T(8,128)(4,1)S(1)}, u32[]{:S(2)}) copy-start(pred[128,1024]{0,1:T(8,128)(4,1)S(1)} %get-tuple-element.13) | copy-start | bytes 393220
  47.3 237.8 %reduce-scatter.3.cloned.1.call-start = ((), (), s32[]{:S(2)}) async-start(), calls=%async_computation.6 | async-start | bytes 1179648 | tf_op jit(solution)/shard_map/reduce_scatter | solution.py:139
  68.3 47.8 %copy-start.33 = (f32[8,128]{1,0:T(8,128)}, f32[8,128]{1,0:T(8,128)S(1)}, u32[]{:S(2)}) copy-start(f32[8,128]{1,0:T(8,128)S(1)} %get-tuple-element.22) | copy-start | bytes 12292
  125.5 3.6 copy-start.11
  125.5 3.6 copy-start.30
  138.8 3.6 copy-start.12
  138.8 3.6 copy-start.31
  149.8 4.6 %copy-start.15 = (f32[8,128,1024]{1,2,0:T(8,128)S(1)}, f32[8,128,1024]{1,2,0:T(8,128)}, u32[]{:S(2)}) copy-start(f32[8,128,1024]{1,2,0:T(8,128)} %get-tuple-element.31) | copy-start | bytes 12582916
  149.8 4.6 %copy-start.34 = (f32[8,128]{1,0:T(8,128)S(1)}, f32[8,128]{1,0:T(8,128)}, u32[]{:S(2)}) copy-start(f32[8,128]{1,0:T(8,128)} %get-tuple-element.30) | copy-start | bytes 12292
  161.1 199.3 %reduce-scatter.5.cloned.1.call-start = ((), (), s32[]{:S(2)}) async-start(), calls=%async_computation.7 | async-start | bytes 1179648 | tf_op jit(solution)/shard_map/reduce_scatter | solution.py:142
  161.1 4.5 %copy-start.8 = (bf16[8,128,1024]{1,2,0:T(8,128)(2,1)S(1)}, bf16[8,128,1024]{1,2,0:T(8,128)(2,1)}, u32[]{:S(2)}) copy-start(bf16[8,128,1024]{1,2,0:T(8,128)(2,1)} %fusion.13) | copy-start | bytes 6291460
  161.1 4.5 %copy-start.23 = (bf16[1024,512]{1,0:T(8,128)(2,1)S(1)}, bf16[1024,512]{1,0:T(8,128)(2,1)}, u32[]{:S(2)}) copy-start(bf16[1024,512]{1,0:T(8,128)(2,1)} %all-gather.9.cloned.1.call-done) | copy-start | bytes 3145732
  161.1 5.0 %copy-start.10 = (bf16[8,128,1024]{1,2,0:T(8,128)(2,1)S(1)}, bf16[8,128,1024]{1,2,0:T(8,128)(2,1)}, u32[]{:S(2)}) copy-start(bf16[8,128,1024]{1,2,0:T(8,128)(2,1)} %copy-done.9) | copy-start | bytes 6291460
  171.1 3.6 copy-start.16
  171.1 3.9 %copy-start.21 = (bf16[1,128,4096]{1,2,0:T(8,128)(2,1)S(1)}, bf16[1,128,4096]{1,2,0:T(8,128)(2,1)}, u32[]{:S(2)}) copy-start(bf16[1,128,4096]{1,2,0:T(8,128)(2,1)} %copy.41) | copy-start | bytes 3145732
  171.1 3.9 %copy-start.35 = (f32[8,128]{1,0:T(8,128)S(1)}, f32[8,128]{1,0:T(8,128)}, u32[]{:S(2)}) copy-start(f32[8,128]{1,0:T(8,128)} %get-tuple-element.30) | copy-start | bytes 12292
  181.8 4.2 %copy-start.3 = (f32[1024,128,8]{1,0,2:T(8,128)}, f32[1024,128,8]{1,0,2:T(8,128)S(1)}, u32[]{:S(2)}) copy-start(f32[1024,128,8]{1,0,2:T(8,128)S(1)} %fusion.151) | copy-start | bytes 12582916
  209.4 3.8 %copy-start.40 = (bf16[1024,512]{1,0:T(8,128)(2,1)S(1)}, bf16[1024,512]{1,0:T(8,128)(2,1)}, u32[]{:S(2)}) copy-start(bf16[1024,512]{1,0:T(8,128)(2,1)} %all-gather.7.cloned.1.call-done) | copy-start | bytes 3145732
  290.8 74.0 %copy-start.37 = (f32[128]{0:T(128)S(1)}, f32[128]{0:T(128)}, u32[]{:S(2)}) copy-start(f32[128]{0:T(128)} %copy-done.36) | copy-start | bytes 1540
  290.9 74.1 %copy-start.38 = (f32[128]{0:T(128)S(1)}, f32[128]{0:T(128)}, u32[]{:S(2)}) copy-start(f32[128]{0:T(128)} %get-tuple-element.11) | copy-start | bytes 1540
  (17 other events, 40.8 us)
Sparse Core Ops, SparseCore 0:
  13.6 49.9 all-gather.8
  65.9 46.8 all-gather.10
  115.2 45.9 all-gather.4
  163.4 45.9 all-gather.6
  213.4 71.6 reduce-scatter.2
  288.6 71.7 reduce-scatter.4
where the time goes:
time: 379 us; the launch traced here: 374 us
  waiting for transfers between devices  215 us (57%)
  matrix products  90.5 us (24%)
  local copies, waits for them, and re-layouts  29.6 us (8%)
  other arithmetic  23.6 us (6%)
  between operations  14.9 us (4%)
    reduce_scatter x1, waiting for transfers between devices, body(): lax.psum_scatter(dvalue_terms.astype(jnp.bfloat16), 'ctx', scatter_dimens...  69.5 us
    reduce_scatter x1, waiting for transfers between devices, body(): lax.psum_scatter(dkey_terms.astype(jnp.bfloat16), 'ctx', scatter_dimensio...  59.2 us
    all_gather x1, waiting for transfers between devices, body(): lax.all_gather(bwd_values, 'ctx', axis=0, tiled=True)  44.6 us
    sub x4, matrix products, body(): expo = jnp.where(allowed[None], jnp.exp(scores - rowmax), 0.0)  21 us
    all_gather x1, waiting for transfers between devices, body(): value_piece = lax.all_gather(fwd_values, 'ctx', axis=0, tiled=True)  18.2 us
    dot_general x4, matrix products, body(): jnp.einsum('tgd,sd->gts', grad_grp, value_grp, preferred_element_type=jnp...  13 us
    unnamed x82, local copies, waits for them, and re-layouts  12.8 us
    ppermute x2, waiting for transfers between devices, shifted(): return lax.ppermute(block, axis, route)  12.7 us
  transfers between devices with their start and end apart: 8, of which 6 were waited for; matrix products, arithmetic and copies ran while one was open for 32% of the time, Pallas kernels for 0%

commit v1 on v0

--- a/solution.py
+++ b/solution.py
@@ -88,7 +88,9 @@
         new_acc.append(product)
     bwd_key_all, bwd_value_all = (
         lax.all_gather(bwd_keys, "ctx", axis=0, tiled=True),
-        lax.all_gather(bwd_values, "ctx", axis=0, tiled=True),
+        jnp.concatenate(
+            lax.all_to_all(jnp.stack([bwd_values] * lax.axis_size("ctx")), "ctx", 0, 0), axis=0
+        ),
     )
     attended = jnp.concatenate(new_acc, axis=0) / jnp.concatenate(new_total, axis=0)[:, :, None]
     attended = jnp.transpose(attended, (1, 0, 2)).reshape(tok_rows, width)

time: 379 us -> 336 us (0.89)
  waiting for transfers between devices: 215 us -> 153 us
  matrix products: 90.5 us -> 99.6 us
  starting transfers between devices: 0.4 us -> 8.31 us
    all_gather x1 -> x0, waiting for transfers between devices: 44.6 us -> none  [body(): lax.all_gather(bwd_values, 'ctx', axis=0, tiled=True)]
    all_gather x1, waiting for transfers between devices: 18.2 us -> 4.13 us  [body(): value_piece = lax.all_gather(fwd_values, 'ctx', axis=0, tiled=True)]
    sub x4, matrix products: 21 us -> 30.7 us  [body(): expo = jnp.where(allowed[None], jnp.exp(scores - rowmax), 0.0)]
    all_to_all x0 -> x1, starting transfers between devices: none -> 7.96 us  [body(): lax.all_to_all(jnp.stack([bwd_values] * lax.axis_size('ctx')), 'ctx', 0, 0)]
    unnamed x82 -> x80, local copies, waits for them, and re-layouts: 12.8 us -> 13 us
  transfers between devices with their start and end apart: 8 -> 8, of which waited for: 6 -> 5; matrix products, arithmetic and copies ran while one was open for 32% -> 41% of each run, Pallas kernels for 0% -> 0%
where the time goes in v1:
time: 336 us; the launch traced here: 330 us
  waiting for transfers between devices  153 us (46%)
  matrix products  99.6 us (30%)
  local copies, waits for them, and re-layouts  30.9 us (9%)
  other arithmetic  23.5 us (7%)
  between operations  14.5 us (4%)
  starting transfers between devices  8.31 us (2%)
    reduce_scatter x1, waiting for transfers between devices, body(): lax.psum_scatter(dvalue_terms.astype(jnp.bfloat16), 'ctx', scatter_dimens...  69.5 us
    reduce_scatter x1, waiting for transfers between devices, body(): lax.psum_scatter(dkey_terms.astype(jnp.bfloat16), 'ctx', scatter_dimensio...  59.2 us
    sub x4, matrix products, body(): expo = jnp.where(allowed[None], jnp.exp(scores - rowmax), 0.0)  30.7 us
    unnamed x80, local copies, waits for them, and re-layouts  13 us
    dot_general x4, matrix products, body(): jnp.einsum('tgd,sd->gts', grad_grp, value_grp, preferred_element_type=jnp...  12.9 us
    ppermute x2, waiting for transfers between devices, shifted(): return lax.ppermute(block, axis, route)  10.4 us
    all_gather x1, waiting for transfers between devices, body(): lax.all_gather(bwd_keys, 'ctx', axis=0, tiled=True)  10 us
    all_to_all x1, starting transfers between devices, body(): lax.all_to_all(jnp.stack([bwd_values] * lax.axis_size('ctx')), 'ctx', 0, 0)  7.96 us
  transfers between devices with their start and end apart: 8, of which 5 were waited for; matrix products, arithmetic and copies ran while one was open for 41% of the time, Pallas kernels for 0%

profile of v1, /device:TPU:0, one launch (start us, length us, event | category | flops | bytes accessed | tf_op | source)
XLA Modules:
  0.0 330.2 jit_solution(15862558604607109155)
XLA Ops:
  9.4 4.0 %fusion.121 = bf16[128,512]{1,0:T(8,128)(2,1)} fusion(bf16[1,4096,512]{2,1,0:T(8,128)(2,1)} %param.12, bf16[1,128,4096]{2,1,0:T(8,128)(2,1)} %param.10, f32[128]{0:T(128)S(1)} %get-tuple-element.12, f32[4096]{0:T(1024)} %bitcast.353), kind=kOutput, calls=%fused_computation.149 | convolution fusion | flops 539033600 | bytes 5390848 | tf_op jit(solution)/shard_map/dot_general | solution.py:42
  13.4 10.4 %collective-permute-done = bf16[1,128,4096]{2,1,0:T(8,128)(2,1)S(1)} collective-permute-done((bf16[1,128,4096]{2,1,0:T(8,128)(2,1)}, bf16[1,128,4096]{2,1,0:T(8,128)(2,1)S(1)}, u32[]{:S(2)}, u32[]{:S(2)}) %collective-permute-start) | collective-permute-done | bytes 1048608 | tf_op jit(solution)/shard_map/ppermute | solution.py:14
  24.1 3.6 %fusion.118 = bf16[128,512]{1,0:T(8,128)(2,1)} fusion(bf16[1,4096,512]{2,1,0:T(8,128)(2,1)} %param.12, bf16[1,128,4096]{2,1,0:T(8,128)(2,1)S(1)} %collective-permute-done, f32[4096]{0:T(1024)S(1)} %bitcast.354, f32[128]{0:T(128)S(1)} %add_rsqrt_fusion.1), kind=kOutput, calls=%fused_computation.148 | convolution fusion | flops 539033600 | bytes 5390848 | tf_op jit(solution)/shard_map/dot_general | solution.py:42
  27.9 3.0 fusion.127
  32.0 8.0 %all-to-all-start = ((bf16[8,128,512]{2,1,0:T(8,128)(2,1)}), bf16[8,128,512]{2,1,0:T(8,128)(2,1)}, u32[]{:S(2)}, u32[]{:S(2)}) async-start(bf16[8,128,512]{2,1,0:T(8,128)(2,1)} %stack.2), calls=%async_computation | async-start | bytes 2097152 | tf_op jit(solution)/shard_map/all_to_all | solution.py:92
  41.7 2.9 copy.40
  45.0 3.8 %fusion.124 = bf16[128,512]{1,0:T(8,128)(2,1)} fusion(bf16[1,4096,512]{2,1,0:T(8,128)(2,1)} %param.13, bf16[1,128,4096]{2,1,0:T(8,128)(2,1)S(1)} %collective-permute-done, f32[4096]{0:T(1024)S(1)} %bitcast.356, f32[128]{0:T(128)S(1)} %add_rsqrt_fusion.1), kind=kOutput, calls=%fused_computation.150 | convolution fusion | flops 539033600 | bytes 5390848 | tf_op jit(solution)/shard_map/dot_general | solution.py:43
  50.4 2.9 copy.29
  55.1 4.2 %multiply_convert_fusion = (bf16[128,32,128]{2,0,1:T(8,128)(2,1)}, bf16[128,32,128]{2,0,1:T(8,128)(2,1)}) fusion(f32[128,32,128]{2,0,1:T(8,128)} %copy.40, f32[128]{0:T(128)S(1)} %get-tuple-element.12, f32[32,128]{1,0:T(8,128)S(1)} %bitcast.357, f32[128,32,128]{2,0,1:T(8,128)} %copy.29, f32[128]{0:T(128)S(1)} %add_rsqrt_fusion.1), kind=kLoop, calls=%fused_computation.95 | loop fusion | flops 3145728 | bytes 6308864 | tf_op jit(solution)/shard_map/convert_element_type | solution.py:41
  59.3 10.0 %all-gather.8.cloned.1.call-done = bf16[1024,512]{1,0:T(8,128)(2,1)} async-done(((bf16[128,512]{1,0:T(8,128)(2,1)}), bf16[1024,512]{1,0:T(8,128)(2,1)}) %all-gather.8.cloned.1.call-update) | async-done | bytes 1048592 | tf_op jit(solution)/shard_map/all_gather | solution.py:90
  69.3 4.7 %fusion.224 = (f32[8,128]{1,0:T(8,128)S(1)}, f32[8,128,1024]{1,2,0:T(8,128)}) fusion(pred[128,1024]{0,1:T(8,128)(4,1)S(1)} %get-tuple-element.13, bf16[128,32,128]{2,0,1:T(8,128)(2,1)} %get-tuple-element.9, bf16[1024,512]{1,0:T(8,128)(2,1)} %all-gather.8.cloned.1.call-done), kind=kOutput, calls=%fused_computation.247 | convolution fusion | flops 273679360 | bytes 4984832 | tf_op jit(solution)/shard_map/sub | solution.py:119
  74.0 3.2 fusion.8
  81.2 5.4 %fusion.219 = (f32[8,128]{1,0:T(8,128)}, f32[8,128,1024]{1,2,0:T(8,128)}) fusion(pred[128,1024]{0,1:T(8,128)(4,1)} %copy-done.26, bf16[128,32,128]{2,0,1:T(8,128)(2,1)} %get-tuple-element.9, bf16[1024,512]{1,0:T(8,128)(2,1)} %all-gather.8.cloned.1.call-done), kind=kOutput, calls=%fused_computation.246 | convolution fusion | flops 273679360 | bytes 4984832 | tf_op jit(solution)/shard_map/sub | solution.py:119
  86.7 3.2 fusion.5
  92.2 2.4 fusion.117
  94.6 5.4 %fusion.229 = (f32[8,128]{1,0:T(8,128)}, f32[8,128,1024]{1,2,0:T(8,128)}) fusion(pred[128,1024]{0,1:T(8,128)(4,1)} %copy-done.26, bf16[128,32,128]{2,0,1:T(8,128)(2,1)} %get-tuple-element.9, bf16[1024,512]{1,0:T(8,128)(2,1)} %all-gather.8.cloned.1.call-done), kind=kOutput, calls=%fused_computation.248 | convolution fusion | flops 273679360 | bytes 4984832 | tf_op jit(solution)/shard_map/sub | solution.py:119
  100.0 3.3 fusion.11
  105.6 15.2 %fusion.234 = (f32[8,128]{1,0:T(8,128)}, f32[8,128,1024]{1,2,0:T(8,128)}) fusion(pred[128,1024]{0,1:T(8,128)(4,1)} %copy-done.26, bf16[128,32,128]{2,0,1:T(8,128)(2,1)} %get-tuple-element.9, bf16[1024,512]{1,0:T(8,128)(2,1)} %all-gather.8.cloned.1.call-done), kind=kOutput, calls=%fused_computation.249 | convolution fusion | flops 273679360 | bytes 4984832 | tf_op jit(solution)/shard_map/sub | solution.py:119
  120.8 3.2 fusion.14
  129.1 3.0 fusion.105
  139.2 3.0 copy.54
  142.2 3.1 fusion.102
  154.0 2.9 fusion.35
  158.9 3.2 fusion.37
  162.1 4.1 %all-gather.6.cloned.1.call-done = bf16[1024,512]{1,0:T(8,128)(2,1)} async-done(((bf16[128,512]{1,0:T(8,128)(2,1)}), bf16[1024,512]{1,0:T(8,128)(2,1)}) %all-gather.6.cloned.1.call-update) | async-done | bytes 1048592 | tf_op jit(solution)/shard_map/all_gather | solution.py:52
  166.2 3.5 %fusion.72 = f32[8,128,128]{1,2,0:T(8,128)S(1)} fusion(f32[1024,128,8]{1,0,2:T(8,128)} %copy-done.19, f32[8,128]{1,0:T(8,128)S(1)} %broadcast_maximum_fusion.3, pred[128,1024]{0,1:T(8,128)(4,1)S(1)} %get-tuple-element.14, bf16[1024,512]{1,0:T(8,128)(2,1)} %all-gather.6.cloned.1.call-done), kind=kOutput, calls=%fused_computation.111 | convolution fusion | flops 273678336 | bytes 5115904 | tf_op jit(solution)/shard_map/gts,sd->gtd/dot_general | solution.py:82
  177.1 2.9 copy.38
  180.1 2.8 add_convert_fusion
  182.8 59.2 %reduce-scatter.3.cloned.1.call-done = bf16[128,512]{1,0:T(8,128)(2,1)} async-done(((bf16[1024,512]{1,0:T(8,128)(2,1)}), bf16[128,512]{1,0:T(8,128)(2,1)}) %reduce-scatter.3.cloned.1.call-update) | async-done | bytes 131088 | tf_op jit(solution)/shard_map/reduce_scatter | solution.py:141
  242.0 5.7 %convolution_add_fusion.1 = f32[128,4096]{1,0:T(8,128)} fusion(f32[128,4096]{1,0:T(8,128)} %copy.54, bf16[128,512]{1,0:T(8,128)(2,1)} %reduce-scatter.3.cloned.1.call-done, bf16[1,4096,512]{2,1,0:T(8,128)(2,1)} %param.12), kind=kOutput, calls=%fused_computation.6 | convolution fusion | flops 537395200 | bytes 8519680 | tf_op jit(solution)/shard_map/dot_general | solution.py:148
  247.8 69.5 %reduce-scatter.5.cloned.1.call-done = bf16[128,512]{1,0:T(8,128)(2,1)} async-done(((bf16[1024,512]{1,0:T(8,128)(2,1)}), bf16[128,512]{1,0:T(8,128)(2,1)}) %reduce-scatter.5.cloned.1.call-update) | async-done | bytes 131088 | tf_op jit(solution)/shard_map/reduce_scatter | solution.py:144
  317.3 4.5 %fusion.47 = (f32[128]{0:T(128)S(1)}, f32[128,4096]{1,0:T(8,128)S(1)}) fusion(bf16[1,128,4096]{2,1,0:T(8,128)(2,1)S(1)} %copy-done, f32[128,4096]{1,0:T(8,128)} %convolution_add_fusion.1, bf16[128,512]{1,0:T(8,128)(2,1)} %reduce-scatter.5.cloned.1.call-done, bf16[1,4096,512]{2,1,0:T(8,128)(2,1)} %param.13, f32[4096]{0:T(1024)S(1)} %bitcast.358), kind=kOutput, calls=%fused_computation.79 | convolution fusion | flops 539492224 | bytes 9585152 | tf_op jit(solution)/shard_map/dot_general | solution.py:151
  (136 shorter events, 49.6 us)
Async XLA Ops:
  7.2 17.0 %copy-start.27 = (f32[1,4096]{1,0:T(1,128)S(1)}, f32[1,4096]{1,0:T(1,128)}, u32[]{:S(2)}) copy-start(f32[1,4096]{1,0:T(1,128)} %param.11) | copy-start | bytes 49156
  7.2 62.2 %all-gather.8.cloned.1.call-start = ((), (), s32[]{:S(2)}) async-start(), calls=%async_computation.5 | async-start | bytes 1179648 | tf_op jit(solution)/shard_map/all_gather | solution.py:90
  7.2 16.6 %collective-permute-start = (bf16[1,128,4096]{2,1,0:T(8,128)(2,1)}, bf16[1,128,4096]{2,1,0:T(8,128)(2,1)S(1)}, u32[]{:S(2)}, u32[]{:S(2)}) collective-permute-start(bf16[1,128,4096]{2,1,0:T(8,128)(2,1)} %param.8), channel_id=1, source_target_pairs={{120,0},{0,8},{8,16},{16,24},{24,32},{32,40},{40,48},{48,56},{56,6... | collective-permute-start | bytes 3145736 | tf_op jit(solution)/shard_map/ppermute | solution.py:14
  9.4 45.7 %copy-start.36 = (f32[128]{0:T(128)}, f32[128]{0:T(128)S(1)}, u32[]{:S(2)}) copy-start(f32[128]{0:T(128)S(1)} %get-tuple-element.12) | copy-start | bytes 1540
  13.3 14.6 %copy-start = (bf16[1,128,4096]{2,1,0:T(8,128)(2,1)S(1)}, bf16[1,128,4096]{2,1,0:T(8,128)(2,1)}, u32[]{:S(2)}) copy-start(bf16[1,128,4096]{2,1,0:T(8,128)(2,1)} %param.10) | copy-start | bytes 3145732
  13.3 136.8 %all-gather.4.cloned.1.call-start = ((), (), s32[]{:S(2)}) async-start(), calls=%async_computation.3 | async-start | bytes 1179648 | tf_op jit(solution)/shard_map/all_gather | solution.py:51
  27.8 25.6 %collective-permute-start.1 = (bf16[1,128,4096]{2,1,0:T(8,128)(2,1)}, bf16[1,128,4096]{2,1,0:T(8,128)(2,1)S(1)}, u32[]{:S(2)}, u32[]{:S(2)}) collective-permute-start(bf16[1,128,4096]{2,1,0:T(8,128)(2,1)} %param.9), channel_id=1, source_target_pairs={{8,0},{16,8},{24,16},{32,24},{40,32},{48,40},{56,48},{64,56},{72,6... | collective-permute-start | bytes 3145736 | tf_op jit(solution)/shard_map/ppermute | solution.py:14
  30.8 10.7 %copy-start.29 = (s32[1024]{0:T(1024)S(1)}, s32[1024]{0:T(1024)}, u32[]{:S(2)}) copy-start(s32[1024]{0:T(1024)} %param.14) | copy-start | bytes 12292
  30.9 10.8 %copy-start.28 = (s32[1024]{0:T(1024)S(1)}, s32[1024]{0:T(1024)}, u32[]{:S(2)}) copy-start(s32[1024]{0:T(1024)} %param.15) | copy-start | bytes 12292
  32.0 42.1 %all-to-all-start = ((bf16[8,128,512]{2,1,0:T(8,128)(2,1)}), bf16[8,128,512]{2,1,0:T(8,128)(2,1)}, u32[]{:S(2)}, u32[]{:S(2)}) async-start(bf16[8,128,512]{2,1,0:T(8,128)(2,1)} %stack.2), calls=%async_computation | async-start | bytes 2097152 | tf_op jit(solution)/shard_map/all_to_all | solution.py:92
  39.9 126.3 %all-gather.6.cloned.1.call-start = ((), (), s32[]{:S(2)}) async-start(), calls=%async_computation.4 | async-start | bytes 1179648 | tf_op jit(solution)/shard_map/all_gather | solution.py:52
  45.0 24.3 %copy-start.26 = (pred[128,1024]{0,1:T(8,128)(4,1)}, pred[128,1024]{0,1:T(8,128)(4,1)S(1)}, u32[]{:S(2)}) copy-start(pred[128,1024]{0,1:T(8,128)(4,1)S(1)} %get-tuple-element.13) | copy-start | bytes 393220
  53.3 188.7 %reduce-scatter.3.cloned.1.call-start = ((), (), s32[]{:S(2)}) async-start(), calls=%async_computation.6 | async-start | bytes 1179648 | tf_op jit(solution)/shard_map/reduce_scatter | solution.py:141
  74.0 3.6 %copy-start.14 = (f32[8,128,1024]{1,2,0:T(8,128)S(1)}, f32[8,128,1024]{1,2,0:T(8,128)}, u32[]{:S(2)}) copy-start(f32[8,128,1024]{1,2,0:T(8,128)} %get-tuple-element.23) | copy-start | bytes 12582916
  86.7 3.6 %copy-start.11 = (f32[8,128,1024]{1,2,0:T(8,128)S(1)}, f32[8,128,1024]{1,2,0:T(8,128)}, u32[]{:S(2)}) copy-start(f32[8,128,1024]{1,2,0:T(8,128)} %get-tuple-element.19) | copy-start | bytes 12582916
  86.7 3.6 %copy-start.30 = (f32[8,128]{1,0:T(8,128)S(1)}, f32[8,128]{1,0:T(8,128)}, u32[]{:S(2)}) copy-start(f32[8,128]{1,0:T(8,128)} %get-tuple-element.18) | copy-start | bytes 12292
  100.0 3.7 %copy-start.12 = (f32[8,128,1024]{1,2,0:T(8,128)S(1)}, f32[8,128,1024]{1,2,0:T(8,128)}, u32[]{:S(2)}) copy-start(f32[8,128,1024]{1,2,0:T(8,128)} %get-tuple-element.27) | copy-start | bytes 12582916
  100.0 3.7 %copy-start.31 = (f32[8,128]{1,0:T(8,128)S(1)}, f32[8,128]{1,0:T(8,128)}, u32[]{:S(2)}) copy-start(f32[8,128]{1,0:T(8,128)} %get-tuple-element.26) | copy-start | bytes 12292
  120.8 4.6 %copy-start.15 = (f32[8,128,1024]{1,2,0:T(8,128)S(1)}, f32[8,128,1024]{1,2,0:T(8,128)}, u32[]{:S(2)}) copy-start(f32[8,128,1024]{1,2,0:T(8,128)} %get-tuple-element.31) | copy-start | bytes 12582916
  120.8 4.6 %copy-start.34 = (f32[8,128]{1,0:T(8,128)S(1)}, f32[8,128]{1,0:T(8,128)}, u32[]{:S(2)}) copy-start(f32[8,128]{1,0:T(8,128)} %get-tuple-element.30) | copy-start | bytes 12292
  132.1 185.2 %reduce-scatter.5.cloned.1.call-start = ((), (), s32[]{:S(2)}) async-start(), calls=%async_computation.7 | async-start | bytes 1179648 | tf_op jit(solution)/shard_map/reduce_scatter | solution.py:144
  132.1 4.5 %copy-start.8 = (bf16[8,128,1024]{1,2,0:T(8,128)(2,1)S(1)}, bf16[8,128,1024]{1,2,0:T(8,128)(2,1)}, u32[]{:S(2)}) copy-start(bf16[8,128,1024]{1,2,0:T(8,128)(2,1)} %fusion.13) | copy-start | bytes 6291460
  132.1 4.5 %copy-start.23 = (bf16[1024,512]{1,0:T(8,128)(2,1)S(1)}, bf16[1024,512]{1,0:T(8,128)(2,1)}, u32[]{:S(2)}) copy-start(bf16[1024,512]{1,0:T(8,128)(2,1)} %all-gather.8.cloned.1.call-done) | copy-start | bytes 3145732
  132.2 5.0 %copy-start.10 = (bf16[8,128,1024]{1,2,0:T(8,128)(2,1)S(1)}, bf16[8,128,1024]{1,2,0:T(8,128)(2,1)}, u32[]{:S(2)}) copy-start(bf16[8,128,1024]{1,2,0:T(8,128)(2,1)} %copy-done.9) | copy-start | bytes 6291460
  142.2 3.5 %copy-start.16 = (f32[8,128,1024]{1,2,0:T(8,128)S(1)}, f32[8,128,1024]{1,2,0:T(8,128)}, u32[]{:S(2)}) copy-start(f32[8,128,1024]{1,2,0:T(8,128)} %get-tuple-element.31) | copy-start | bytes 12582916
  142.2 3.8 %copy-start.21 = (bf16[1,128,4096]{1,2,0:T(8,128)(2,1)S(1)}, bf16[1,128,4096]{1,2,0:T(8,128)(2,1)}, u32[]{:S(2)}) copy-start(bf16[1,128,4096]{1,2,0:T(8,128)(2,1)} %copy.41) | copy-start | bytes 3145732
  142.2 3.8 %copy-start.35 = (f32[8,128]{1,0:T(8,128)S(1)}, f32[8,128]{1,0:T(8,128)}, u32[]{:S(2)}) copy-start(f32[8,128]{1,0:T(8,128)} %get-tuple-element.30) | copy-start | bytes 12292
  152.8 4.2 %copy-start.3 = (f32[1024,128,8]{1,0,2:T(8,128)}, f32[1024,128,8]{1,0,2:T(8,128)S(1)}, u32[]{:S(2)}) copy-start(f32[1024,128,8]{1,0,2:T(8,128)S(1)} %fusion.151) | copy-start | bytes 12582916
  166.2 3.5 %copy-start.4 = (f32[1024,128,8]{1,0,2:T(8,128)S(1)}, f32[1024,128,8]{1,0,2:T(8,128)}, u32[]{:S(2)}) copy-start(f32[1024,128,8]{1,0,2:T(8,128)} %copy-done.3) | copy-start | bytes 12582916
  166.2 3.8 %copy-start.39 = (bf16[1024,512]{1,0:T(8,128)(2,1)S(1)}, bf16[1024,512]{1,0:T(8,128)(2,1)}, u32[]{:S(2)}) copy-start(bf16[1024,512]{1,0:T(8,128)(2,1)} %all-gather.6.cloned.1.call-done) | copy-start | bytes 3145732
  247.8 74.0 %copy-start.37 = (f32[128]{0:T(128)S(1)}, f32[128]{0:T(128)}, u32[]{:S(2)}) copy-start(f32[128]{0:T(128)} %copy-done.36) | copy-start | bytes 1540
  247.8 74.0 %copy-start.38 = (f32[128]{0:T(128)S(1)}, f32[128]{0:T(128)}, u32[]{:S(2)}) copy-start(f32[128]{0:T(128)} %get-tuple-element.11) | copy-start | bytes 1540
  (16 other events, 36.5 us)
Sparse Core Ops, SparseCore 0:
  13.5 55.8 all-gather.7
  71.7 46.2 all-gather.3
  120.3 45.9 all-gather.5
  170.3 71.6 reduce-scatter.2
  245.5 71.7 reduce-scatter.4
